TPU v7x, 32 devices: a whole 2x2x4 slice. The times are simulated.
32 devices in a mesh: img: 8 (over z, core), slab: 4 (over y, x).
Axes of the slice: x: 2, y: 2, z: 4, core: 2. Of those that a mesh axis runs over, the one named last changes fastest.
Arguments:
- image_masses: float32 [8, 3072, 3072], P('img', 'slab'), may hold values from 0.1 to 10
- dual_multipliers: float32 [8, 3072, 3072], P('img', 'slab'), may hold values from 0.1 to 10
- fraction_tops: int32 [8], P('img'), may hold values from 1 to 8
- banded_submatrices: bfloat16 [24, 3, 128, 128], replicated, as said below
- band_starts: int32 [24, 3], replicated, may hold values from -2 to 2, as said below
Outputs:
- barycenter: float32 [3072, 3072], P('slab')
- new_scalings: float32 [8, 3072, 3072], P('img', 'slab')
Inputs may be any that keep to these rules, and one draw needn't show every extreme that they name: `band_starts`: each row of offsets holds three consecutive numbers in increasing order; the first row is 0, 1, 2 and the last row is -2, -1, 0. `banded_submatrices`: all entries are positive.
All inputs are finite; a program needn't handle non-finite values.
Results may differ from a plain program's by a relative error of at most 0.0032.
Values may be sent and summed in bfloat16 or wider, within the bound.
No kernel may reach another device: no remote copies, remote signals or barrier semaphores. Data moves between devices by JAX's collectives and lax.ppermute only.
A program may use at most 192 MiB of HBM per device.

v0:
```python
import jax
import jax.numpy as jnp
from jax import lax
from jax.sharding import PartitionSpec as P

ITERS = 2


def offset_terms(banded_submatrices, band_starts):
    offsets = jnp.arange(-2, 3, dtype=jnp.int32)
    matches = band_starts[:, None, :] == offsets[None, :, None]
    picked = jnp.where(
        matches[:, :, :, None, None], banded_submatrices[:, None], jnp.zeros((), jnp.bfloat16)
    )
    return jnp.sum(picked, axis=2)


def column_sweep(field, terms):
    block_stack = terms.shape[0]
    width = terms.shape[2]
    count = field.shape[0]
    height = field.shape[1]
    leading = field.reshape((count * height, block_stack, width)).transpose(1, 0, 2)
    padded = jnp.pad(leading, ((2, 2), (0, 0), (0, 0)))
    total = jnp.zeros((block_stack, count * height, width), jnp.float32)
    for offset in range(5):
        total = total + lax.dot_general(
            padded[offset : offset + block_stack],
            terms[:, offset],
            (((2,), (2,)), ((0,), (0,))),
            preferred_element_type=jnp.float32,
        )
    return total.transpose(1, 0, 2).reshape((count, height, block_stack * width))


def rows_pass(padded, terms):
    block_stack = terms.shape[0]
    width = terms.shape[2]
    columns = padded.shape[2]
    split = padded[0].reshape((block_stack + 4, width, columns))
    total = jnp.zeros((block_stack, width, columns), jnp.float32)
    for offset in range(5):
        total = total + lax.dot_general(
            terms[:, offset],
            split[offset : offset + block_stack],
            (((2,), (1,)), ((0,), (0,))),
            preferred_element_type=jnp.float32,
        )
    outputs = [total.reshape((block_stack * width, columns))]
    return jnp.stack(outputs, axis=0)


def per_device(image_masses, dual_multipliers, fraction_tops, banded_submatrices, band_starts):
    width = banded_submatrices.shape[2]
    terms = offset_terms(banded_submatrices, band_starts)
    total_weight = lax.psum(jnp.sum(fraction_tops).astype(jnp.float32), "img")
    weights = fraction_tops.astype(jnp.float32)

    def apply_kernel(field):
        inner = column_sweep(field, terms).astype(jnp.bfloat16)
        columns = lax.all_to_all(inner, "slab", split_axis=2, concat_axis=1, tiled=True)
        padded = jnp.pad(columns, ((0, 0), (2 * width, 2 * width), (0, 0)))
        result = rows_pass(padded, terms).astype(jnp.bfloat16)
        return lax.all_to_all(result, "slab", split_axis=1, concat_axis=2, tiled=True)

    latest_multiplier = dual_multipliers
    barycenter = jnp.zeros(image_masses.shape[1:], jnp.float32)
    for iteration in range(ITERS):
        kernel_v = apply_kernel(latest_multiplier.astype(jnp.bfloat16))
        scaled_u = (image_masses / kernel_v.astype(jnp.float32)).astype(jnp.bfloat16)
        kernel_u = apply_kernel(scaled_u)
        value_portion = jnp.einsum("i,irc->rc", weights, jnp.log(kernel_u.astype(jnp.float32)))
        barycenter = jnp.exp(lax.psum(value_portion, "img") / total_weight)
        latest_multiplier = barycenter[None] / kernel_u.astype(jnp.float32)
    return (barycenter, latest_multiplier)


def solution(mesh):
    placed = (P("img", "slab", None), P("img", "slab", None), P("img"), P(), P())
    return jax.shard_map(
        per_device,
        mesh=mesh,
        in_specs=placed,
        out_specs=(P("slab", None), P("img", "slab", None)),
        check_vma=False,
    )
```

profile of v0, /device:TPU:0, one launch (start us, length us, event | category | flops | bytes accessed | tf_op | source)
XLA Modules:
  0.0 2068.6 jit_solution(6369687439953317268)
XLA Ops:
  50.3 16.8 fusion.3
  77.7 49.0 %reduce.1 = bf16[3072,768]{1,0:T(8,128)(2,1)} reduce(bf16[3072,1,768]{2,1,0:T(2,128)(2,1)} %bitcast.287, bf16[]{:T(256)} %broadcast.49), dimensions={1}, to_apply=%bitcast.273.reduce_sub_computation | reduce | bytes 9437186
  132.1 61.0 %all_to_all.108 = bf16[4,2,294912]{2,1,0:T(2,128)(2,1)} all-to-all(bf16[4,2,294912]{2,1,0:T(2,128)(2,1)} %reshape.244), channel_id=1, replica_groups=mesh['img'=8,'slab'=4] {'slab'}, dimensions={0} | all-to-all | bytes 9437184 | tf_op jit(solution)/shard_map/all_to_all | solution.py:61
  241.3 18.2 add_convert_fusion.6
  269.0 49.2 %reduce.2 = bf16[3072,768]{1,0:T(8,128)(2,1)} reduce(bf16[3072,1,768]{2,1,0:T(2,128)(2,1)} %bitcast.290, bf16[]{:T(256)} %broadcast.49), dimensions={1}, to_apply=%bitcast.272.reduce_sub_computation | reduce | bytes 9437186
  338.2 42.8 %all-to-all-done.1 = bf16[4,2,294912]{2,1,0:T(2,128)(2,1)} async-done(((bf16[4,2,294912]{2,1,0:T(2,128)(2,1)}), bf16[4,2,294912]{2,1,0:T(2,128)(2,1)}, u32[]{:S(2)}, u32[]{:S(2)}) %all-to-all-start.1) | async-done | bytes 4718624 | tf_op jit(solution)/shard_map/all_to_all | solution.py:64
  389.0 23.5 %copy.138 = f32[1,4,768,768]{2,3,1,0:T(8,128)} copy(bf16[1,4,768,768]{3,0,2,1:T(2,128)(2,1)} %bitcast.291) | data formatting | bytes 14155776 | tf_op jit(solution)/shard_map/convert_element_type | solution.py:70
  452.1 16.8 add_convert_fusion.5
  478.4 49.4 %reduce.3 = bf16[3072,768]{1,0:T(8,128)(2,1)} reduce(bf16[3072,1,768]{2,1,0:T(2,128)(2,1)} %bitcast.292, bf16[]{:T(256)} %broadcast.49), dimensions={1}, to_apply=%bitcast.271.reduce_sub_computation | reduce | bytes 9437186
  533.1 58.9 %all_to_all.109 = bf16[4,2,294912]{2,1,0:T(2,128)(2,1)} all-to-all(bf16[4,2,294912]{2,1,0:T(2,128)(2,1)} %reshape.248), channel_id=1, replica_groups=mesh['img'=8,'slab'=4] {'slab'}, dimensions={0} | all-to-all | bytes 9437184 | tf_op jit(solution)/shard_map/all_to_all | solution.py:61
  640.1 18.1 add_convert_fusion.4
  667.7 49.1 %reduce.4 = bf16[3072,768]{1,0:T(8,128)(2,1)} reduce(bf16[3072,1,768]{2,1,0:T(2,128)(2,1)} %bitcast.294, bf16[]{:T(256)} %broadcast.49), dimensions={1}, to_apply=%bitcast.270.reduce_sub_computation | reduce | bytes 9437186
  727.9 50.3 %all-to-all-done.3 = bf16[4,2,294912]{2,1,0:T(2,128)(2,1)} async-done(((bf16[4,2,294912]{2,1,0:T(2,128)(2,1)}), bf16[4,2,294912]{2,1,0:T(2,128)(2,1)}, u32[]{:S(2)}, u32[]{:S(2)}) %all-to-all-start.3) | async-done | bytes 4718624 | tf_op jit(solution)/shard_map/all_to_all | solution.py:64
  801.7 23.3 %copy.145 = f32[1,4,768,768]{2,3,1,0:T(8,128)} copy(f32[1,4,768,768]{3,0,2,1:T(1,128)} %bitcast.302) | data formatting | bytes 18874368 | tf_op jit(solution)/shard_map/i,irc->rc/dot_general | solution.py:72
  825.0 16.9 psum.22
  841.9 23.6 %copy.146 = f32[1,4,768,768]{2,3,1,0:T(8,128)} copy(bf16[1,4,768,768]{3,0,2,1:T(2,128)(2,1)} %bitcast.274) | data formatting | bytes 14155776 | tf_op jit(solution)/shard_map/convert_element_type | solution.py:72
  865.5 155.0 %all-reduce.11.cloned.1.call-done = f32[768,3072]{0,1:T(8,128)} async-done(((f32[768,3072]{0,1:T(8,128)}), f32[768,3072]{0,1:T(8,128)}) %all-reduce.11.cloned.1.call-update) | async-done | bytes 9437200 | tf_op jit(solution)/shard_map/psum | solution.py:73
  1086.8 49.4 %reduce.5 = bf16[3072,768]{1,0:T(8,128)(2,1)} reduce(bf16[3072,1,768]{2,1,0:T(2,128)(2,1)} %bitcast.295, bf16[]{:T(256)} %broadcast.49), dimensions={1}, to_apply=%bitcast.269.reduce_sub_computation | reduce | bytes 9437186
  1141.6 59.5 %all_to_all.110 = bf16[4,2,294912]{2,1,0:T(2,128)(2,1)} all-to-all(bf16[4,2,294912]{2,1,0:T(2,128)(2,1)} %reshape.252), channel_id=1, replica_groups=mesh['img'=8,'slab'=4] {'slab'}, dimensions={0} | all-to-all | bytes 9437184 | tf_op jit(solution)/shard_map/all_to_all | solution.py:61
  1249.2 18.1 add_convert_fusion.2
  1276.9 49.1 %reduce.6 = bf16[3072,768]{1,0:T(8,128)(2,1)} reduce(bf16[3072,1,768]{2,1,0:T(2,128)(2,1)} %bitcast.297, bf16[]{:T(256)} %broadcast.49), dimensions={1}, to_apply=%bitcast.268.reduce_sub_computation | reduce | bytes 9437186
  1331.4 58.2 %all_to_all.111 = bf16[4,2,294912]{2,1,0:T(2,128)(2,1)} all-to-all(bf16[4,2,294912]{2,1,0:T(2,128)(2,1)} %reshape.254), channel_id=1, replica_groups=mesh['img'=8,'slab'=4] {'slab'}, dimensions={0} | all-to-all | bytes 9437184 | tf_op jit(solution)/shard_map/all_to_all | solution.py:64
  1397.6 23.5 %copy.152 = f32[1,4,768,768]{2,3,1,0:T(8,128)} copy(bf16[1,4,768,768]{3,0,2,1:T(2,128)(2,1)} %bitcast.298) | data formatting | bytes 14155776 | tf_op jit(solution)/shard_map/convert_element_type | solution.py:70
  1460.6 16.8 add_convert_fusion.1
  1486.9 49.4 %reduce.7 = bf16[3072,768]{1,0:T(8,128)(2,1)} reduce(bf16[3072,1,768]{2,1,0:T(2,128)(2,1)} %bitcast.299, bf16[]{:T(256)} %broadcast.49), dimensions={1}, to_apply=%bitcast.267.reduce_sub_computation | reduce | bytes 9437186
  1541.8 56.8 %all_to_all.112 = bf16[4,2,294912]{2,1,0:T(2,128)(2,1)} all-to-all(bf16[4,2,294912]{2,1,0:T(2,128)(2,1)} %reshape.256), channel_id=1, replica_groups=mesh['img'=8,'slab'=4] {'slab'}, dimensions={0} | all-to-all | bytes 9437184 | tf_op jit(solution)/shard_map/all_to_all | solution.py:61
  1646.7 18.2 add_convert_fusion
  1674.4 49.2 %reduce.8 = bf16[3072,768]{1,0:T(8,128)(2,1)} reduce(bf16[3072,1,768]{2,1,0:T(2,128)(2,1)} %bitcast.288, bf16[]{:T(256)} %broadcast.49), dimensions={1}, to_apply=%bitcast.266.reduce_sub_computation | reduce | bytes 9437186
  1729.0 55.4 %all_to_all.113 = bf16[4,2,294912]{2,1,0:T(2,128)(2,1)} all-to-all(bf16[4,2,294912]{2,1,0:T(2,128)(2,1)} %reshape.258), channel_id=1, replica_groups=mesh['img'=8,'slab'=4] {'slab'}, dimensions={0} | all-to-all | bytes 9437184 | tf_op jit(solution)/shard_map/all_to_all | solution.py:64
  1807.7 23.3 %copy.159 = f32[1,4,768,768]{2,3,1,0:T(8,128)} copy(f32[1,4,768,768]{3,0,2,1:T(1,128)} %bitcast.301) | data formatting | bytes 18874368 | tf_op jit(solution)/shard_map/i,irc->rc/dot_general | solution.py:72
  1831.0 23.5 %copy.160 = f32[1,4,768,768]{2,3,1,0:T(8,128)} copy(bf16[1,4,768,768]{3,0,2,1:T(2,128)(2,1)} %bitcast.275) | data formatting | bytes 14155776 | tf_op jit(solution)/shard_map/convert_element_type | solution.py:72
  1854.5 172.9 %all-reduce.13.cloned.1.call-done = f32[768,3072]{0,1:T(8,128)} async-done(((f32[768,3072]{0,1:T(8,128)}), f32[768,3072]{0,1:T(8,128)}) %all-reduce.13.cloned.1.call-update) | async-done | bytes 9437200 | tf_op jit(solution)/shard_map/psum | solution.py:73
  (128 shorter events, 608.5 us)
Async XLA Ops:
  15.6 6.9 copy-start.16
  26.3 18.9 copy-start
  26.3 8.9 copy-start.12
  214.4 7.8 copy-start.8
  222.3 3.8 copy-start.1
  323.6 57.3 %all-to-all-start.1 = ((bf16[4,2,294912]{2,1,0:T(2,128)(2,1)}), bf16[4,2,294912]{2,1,0:T(2,128)(2,1)}, u32[]{:S(2)}, u32[]{:S(2)}) async-start(bf16[4,2,294912]{2,1,0:T(2,128)(2,1)} %reshape.246), calls=%async_computation.1 | async-start | bytes 9437184 | tf_op jit(solution)/shard_map/all_to_all | solution.py:64
  429.2 7.7 copy-start.2
  429.2 7.7 copy-start.13
  613.3 7.7 copy-start.9
  621.0 3.8 copy-start.3
  722.3 56.0 %all-to-all-start.3 = ((bf16[4,2,294912]{2,1,0:T(2,128)(2,1)}), bf16[4,2,294912]{2,1,0:T(2,128)(2,1)}, u32[]{:S(2)}, u32[]{:S(2)}) async-start(bf16[4,2,294912]{2,1,0:T(2,128)(2,1)} %reshape.250), calls=%async_computation.3 | async-start | bytes 9437184 | tf_op jit(solution)/shard_map/all_to_all | solution.py:64
  727.2 293.3 %all-reduce.11.cloned.1.call-start = ((), (), s32[]{:S(2)}) async-start(), calls=%async_computation.8 | async-start | bytes 18874368 | tf_op jit(solution)/shard_map/psum | solution.py:73
  824.9 1202.4 %all-reduce.13.cloned.1.call-start = ((), (), s32[]{:S(2)}) async-start(), calls=%async_computation.9 | async-start | bytes 18874368 | tf_op jit(solution)/shard_map/psum | solution.py:73
  1037.6 7.7 copy-start.4
  1037.6 7.7 copy-start.14
  1222.4 7.7 copy-start.10
  1230.1 3.8 copy-start.5
  1437.7 7.8 copy-start.6
  1437.7 7.8 copy-start.15
  1619.9 7.8 copy-start.11
  1627.7 3.8 copy-start.7
Sparse Core Ops, SparseCore 0:
  825.1 195.3 all-reduce.10
  1831.1 196.2 all-reduce.12
where the time goes:
time: 2080 us; the launch traced here: 2070 us
  other arithmetic  474 us (23%)
  local copies, waits for them, and re-layouts  458 us (22%)
  waiting for transfers between devices  421 us (20%)
  blocking collectives  367 us (18%)
  matrix products  324 us (16%)
    unnamed x8, other arithmetic  394 us
    psum x2, waiting for transfers between devices, per_device(): barycenter = jnp.exp(lax.psum(value_portion, 'img') / total_weight)  328 us
    all_to_all x4, blocking collectives, apply_kernel(): lax.all_to_all(inner, 'slab', split_axis=2, concat_axis=1, tiled=True)  236 us
    unnamed x60, local copies, waits for them, and re-layouts  174 us
    dot_general x20, matrix products, rows_pass(): lax.dot_general(terms[:, offset], split[offset:offset + block_stack], (((...  165 us
    dot_general x20, matrix products, column_sweep(): lax.dot_general(padded[offset:offset + block_stack], terms[:, offset], ((...  160 us
    all_to_all x2, blocking collectives, apply_kernel(): lax.all_to_all(result, 'slab', split_axis=1, concat_axis=2, tiled=True)  114 us
    all_to_all x2, waiting for transfers between devices, apply_kernel(): lax.all_to_all(result, 'slab', split_axis=1, concat_axis=2, tiled=True)  93.1 us
  transfers between devices with their start and end apart: 4, of which 4 were waited for; matrix products, arithmetic and copies ran while one was open for 3% of the time, Pallas kernels for 0%

commit v1 on v0

--- a/solution.py
+++ b/solution.py
@@ -4,6 +4,18 @@
 from jax.sharding import PartitionSpec as P
 
 ITERS = 2
+
+
+def split_up(x, dim, length):
+    shape = x.shape
+    pieces = x.reshape(*shape[:dim], length, shape[dim] // length, *shape[dim + 1 :])
+    return jnp.moveaxis(pieces, dim, 0)
+
+
+def joined_along(parts, dim):
+    lengths = list(parts.shape[1:])
+    lengths[dim] *= parts.shape[0]
+    return jnp.moveaxis(parts, 0, dim).reshape(lengths)
 
 
 def offset_terms(banded_submatrices, band_starts):
@@ -58,7 +70,14 @@
 
     def apply_kernel(field):
         inner = column_sweep(field, terms).astype(jnp.bfloat16)
-        columns = lax.all_to_all(inner, "slab", split_axis=2, concat_axis=1, tiled=True)
+        count_2, index = (lax.axis_size("slab"), lax.axis_index("slab"))
+        blocks = split_up(inner, 2, count_2)
+        outs = [blocks[index]]
+        for step in range(1, count_2):
+            sent = blocks[index ^ step]
+            outs.append(lax.ppermute(sent, "slab", [(i, i ^ step) for i in range(count_2)]))
+        blocks = jnp.stack(outs)[index ^ jnp.arange(count_2)]
+        columns = joined_along(blocks, 1)
         padded = jnp.pad(columns, ((0, 0), (2 * width, 2 * width), (0, 0)))
         result = rows_pass(padded, terms).astype(jnp.bfloat16)
         return lax.all_to_all(result, "slab", split_axis=1, concat_axis=2, tiled=True)

time: 2080 us -> 1800 us (0.87)
  blocking collectives: 367 us -> 134 us
  waiting for transfers between devices: 421 us -> 614 us
  other arithmetic: 474 us -> 291 us
  local copies, waits for them, and re-layouts: 458 us -> 389 us
    all_to_all x4 -> x0, blocking collectives: 236 us -> none  [apply_kernel(): lax.all_to_all(inner, 'slab', split_axis=2, concat_axis=1, tiled=True)]
    unnamed x8 -> x4, other arithmetic: 394 us -> 196 us
    ppermute x0 -> x12, waiting for transfers between devices: none -> 195 us  [apply_kernel(): lax.ppermute(sent, 'slab', [(i, i ^ step) for i in range(count_2)])]
    unnamed x60 -> x42, local copies, waits for them, and re-layouts: 174 us -> 91.9 us
    convert_element_type x4 -> x0, local copies, waits for them, and re-layouts: 38.6 us -> none  [apply_kernel(): inner = column_sweep(field, terms).astype(jnp.bfloat16)]
    another operation x0 -> x20, local copies, waits for them, and re-layouts: none -> 38.4 us
    all_to_all x4 -> x0, local copies, waits for them, and re-layouts: 26.4 us -> none  [apply_kernel(): lax.all_to_all(inner, 'slab', split_axis=2, concat_axis=1, tiled=True)]
    gather x0 -> x4, local copies, waits for them, and re-layouts: none -> 21.8 us  [apply_kernel(): blocks = jnp.stack(outs)[index ^ jnp.arange(count_2)]]
  transfers between devices with their start and end apart: 4 -> 16, of which waited for: 4 -> 13; matrix products, arithmetic and copies ran while one was open for 3% -> 3% of each run, Pallas kernels for 0% -> 0%
where the time goes in v1:
time: 1800 us; the launch traced here: 1780 us
  waiting for transfers between devices  614 us (34%)
  local copies, waits for them, and re-layouts  389 us (22%)
  matrix products  314 us (17%)
  other arithmetic  291 us (16%)
  blocking collectives  134 us (7%)
  starting transfers between devices  25.3 us (1%)
    psum x2, waiting for transfers between devices, per_device(): barycenter = jnp.exp(lax.psum(value_portion, 'img') / total_weight)  326 us
    unnamed x4, other arithmetic  196 us
    ppermute x12, waiting for transfers between devices, apply_kernel(): lax.ppermute(sent, 'slab', [(i, i ^ step) for i in range(count_2)])  195 us
    dot_general x20, matrix products, column_sweep(): lax.dot_general(padded[offset:offset + block_stack], terms[:, offset], ((...  160 us
    dot_general x20, matrix products, rows_pass(): lax.dot_general(terms[:, offset], split[offset:offset + block_stack], (((...  154 us
    all_to_all x2, blocking collectives, apply_kernel(): lax.all_to_all(result, 'slab', split_axis=1, concat_axis=2, tiled=True)  115 us
    all_to_all x2, waiting for transfers between devices, apply_kernel(): lax.all_to_all(result, 'slab', split_axis=1, concat_axis=2, tiled=True)  92.6 us
    unnamed x42, local copies, waits for them, and re-layouts  91.9 us
  transfers between devices with their start and end apart: 16, of which 13 were waited for; matrix products, arithmetic and copies ran while one was open for 3% of the time, Pallas kernels for 0%

profile of v1, /device:TPU:0, one launch (start us, length us, event | category | flops | bytes accessed | tf_op | source)
XLA Modules:
  0.0 1782.8 jit_solution(8484849492822830462)
XLA Ops:
  81.4 21.9 %collective-permute-done = bf16[1,768,768]{2,1,0:T(8,128)(2,1)} collective-permute-done((bf16[1,768,768]{2,1,0:T(8,128)(2,1)}, bf16[1,768,768]{2,1,0:T(8,128)(2,1)}, u32[]{:S(2)}, u32[]{:S(2)}) %collective-permute-start) | collective-permute-done | bytes 1179680 | tf_op jit(solution)/shard_map/ppermute | solution.py:78
  103.2 27.4 %collective-permute-done.1 = bf16[1,768,768]{2,1,0:T(8,128)(2,1)S(1)} collective-permute-done((bf16[1,768,768]{2,1,0:T(8,128)(2,1)}, bf16[1,768,768]{2,1,0:T(8,128)(2,1)S(1)}, u32[]{:S(2)}, u32[]{:S(2)}) %collective-permute-start.1) | collective-permute-done | bytes 1179680 | tf_op jit(solution)/shard_map/ppermute | solution.py:78
  167.9 18.2 %add_convert_fusion.6 = bf16[24,128,768]{2,1,0:T(8,128)(2,1)} fusion(f32[24,128,768]{2,1,0:T(8,128)} %fusion.67, f32[24,128,768]{2,1,0:T(8,128)} %fusion.63, f32[24,128,768]{2,1,0:T(8,128)} %fusion.55, f32[24,128,768]{2,1,0:T(8,128)} %fusion.59, bf16[24,128,768]{2,1,0:T(8,128)(2,1)} %bitcast.289, bf16[24,5,128,128]{3,2,1,0:T(8,128)(2,1)} %copy-done), kind=kOutput, calls=%fused_computation.25 | convolution fusion | flops 615776256 | bytes 47972352 | tf_op jit(solution)/shard_map/dot_general | solution.py:55
  196.2 49.0 %reduce.1 = bf16[3072,768]{1,0:T(8,128)(2,1)} reduce(bf16[3072,1,768]{2,1,0:T(2,128)(2,1)} %bitcast.297, bf16[]{:T(256)} %broadcast.90), dimensions={1}, to_apply=%bitcast.283.reduce_sub_computation | reduce | bytes 9437186
  265.6 42.5 %all-to-all-done = bf16[4,2,294912]{2,1,0:T(2,128)(2,1)} async-done(((bf16[4,2,294912]{2,1,0:T(2,128)(2,1)}), bf16[4,2,294912]{2,1,0:T(2,128)(2,1)}, u32[]{:S(2)}, u32[]{:S(2)}) %all-to-all-start) | async-done | bytes 4718624 | tf_op jit(solution)/shard_map/all_to_all | solution.py:83
  316.2 23.6 %copy.95 = f32[1,4,768,768]{2,3,1,0:T(8,128)} copy(bf16[1,4,768,768]{3,0,2,1:T(2,128)(2,1)} %bitcast.299) | data formatting | bytes 14155776 | tf_op jit(solution)/shard_map/convert_element_type | solution.py:89
  379.3 16.8 add_convert_fusion.5
  409.2 25.0 %collective-permute-done.3 = bf16[1,768,768]{2,1,0:T(8,128)(2,1)S(1)} collective-permute-done((bf16[1,768,768]{2,1,0:T(8,128)(2,1)}, bf16[1,768,768]{2,1,0:T(8,128)(2,1)S(1)}, u32[]{:S(2)}, u32[]{:S(2)}) %collective-permute-start.3) | collective-permute-done | bytes 1179680 | tf_op jit(solution)/shard_map/ppermute | solution.py:78
  434.2 23.4 %collective-permute-done.4 = bf16[1,768,768]{2,1,0:T(8,128)(2,1)} collective-permute-done((bf16[1,768,768]{2,1,0:T(8,128)(2,1)}, bf16[1,768,768]{2,1,0:T(8,128)(2,1)}, u32[]{:S(2)}, u32[]{:S(2)}) %collective-permute-start.4) | collective-permute-done | bytes 1179680 | tf_op jit(solution)/shard_map/ppermute | solution.py:78
  495.1 18.2 %add_convert_fusion.4 = bf16[24,128,768]{2,1,0:T(8,128)(2,1)} fusion(f32[24,128,768]{2,1,0:T(8,128)} %fusion.66, f32[24,128,768]{2,1,0:T(8,128)} %fusion.62, f32[24,128,768]{2,1,0:T(8,128)} %fusion.54, f32[24,128,768]{2,1,0:T(8,128)} %fusion.58, bf16[24,128,768]{2,1,0:T(8,128)(2,1)} %bitcast.291, bf16[24,5,128,128]{3,2,1,0:T(8,128)(2,1)} %copy-done), kind=kOutput, calls=%fused_computation.23 | convolution fusion | flops 615776256 | bytes 47972352 | tf_op jit(solution)/shard_map/dot_general | solution.py:55
  522.8 49.0 %reduce.2 = bf16[3072,768]{1,0:T(8,128)(2,1)} reduce(bf16[3072,1,768]{2,1,0:T(2,128)(2,1)} %bitcast.300, bf16[]{:T(256)} %broadcast.90), dimensions={1}, to_apply=%bitcast.282.reduce_sub_computation | reduce | bytes 9437186
  582.9 50.1 %all-to-all-done.1 = bf16[4,2,294912]{2,1,0:T(2,128)(2,1)} async-done(((bf16[4,2,294912]{2,1,0:T(2,128)(2,1)}), bf16[4,2,294912]{2,1,0:T(2,128)(2,1)}, u32[]{:S(2)}, u32[]{:S(2)}) %all-to-all-start.1) | async-done | bytes 4718624 | tf_op jit(solution)/shard_map/all_to_all | solution.py:83
  656.4 23.3 %copy.103 = f32[1,4,768,768]{2,3,1,0:T(8,128)} copy(f32[1,4,768,768]{3,0,2,1:T(1,128)} %bitcast.304) | data formatting | bytes 18874368 | tf_op jit(solution)/shard_map/i,irc->rc/dot_general | solution.py:91
  679.8 18.8 %psum.22 = f32[]{:T(128)} all-reduce(f32[]{:T(128)} %bitcast.51), channel_id=1, replica_groups=mesh['img'=8,'slab'=4] {'img'}, use_global_device_ids=true, to_apply=%region_2.3 | all-reduce | flops 1 | bytes 8 | tf_op jit(solution)/shard_map/psum | solution.py:68
  698.5 23.6 %copy.104 = f32[1,4,768,768]{2,3,1,0:T(8,128)} copy(bf16[1,4,768,768]{3,0,2,1:T(2,128)(2,1)} %bitcast.284) | data formatting | bytes 14155776 | tf_op jit(solution)/shard_map/convert_element_type | solution.py:91
  722.2 153.9 %all-reduce.11.cloned.1.call-done = f32[768,3072]{0,1:T(8,128)} async-done(((f32[768,3072]{0,1:T(8,128)}), f32[768,3072]{0,1:T(8,128)}) %all-reduce.11.cloned.1.call-update) | async-done | bytes 9437200 | tf_op jit(solution)/shard_map/psum | solution.py:92
  916.0 16.8 add_convert_fusion.3
  945.9 25.0 %collective-permute-done.6 = bf16[1,768,768]{2,1,0:T(8,128)(2,1)S(1)} collective-permute-done((bf16[1,768,768]{2,1,0:T(8,128)(2,1)}, bf16[1,768,768]{2,1,0:T(8,128)(2,1)S(1)}, u32[]{:S(2)}, u32[]{:S(2)}) %collective-permute-start.6) | collective-permute-done | bytes 1179680 | tf_op jit(solution)/shard_map/ppermute | solution.py:78
  970.8 25.2 %collective-permute-done.7 = bf16[1,768,768]{2,1,0:T(8,128)(2,1)} collective-permute-done((bf16[1,768,768]{2,1,0:T(8,128)(2,1)}, bf16[1,768,768]{2,1,0:T(8,128)(2,1)}, u32[]{:S(2)}, u32[]{:S(2)}) %collective-permute-start.7) | collective-permute-done | bytes 1179680 | tf_op jit(solution)/shard_map/ppermute | solution.py:78
  1033.6 18.2 %add_convert_fusion.2 = bf16[24,128,768]{2,1,0:T(8,128)(2,1)} fusion(f32[24,128,768]{2,1,0:T(8,128)} %fusion.65, f32[24,128,768]{2,1,0:T(8,128)} %fusion.61, f32[24,128,768]{2,1,0:T(8,128)} %fusion.53, f32[24,128,768]{2,1,0:T(8,128)} %fusion.57, bf16[24,128,768]{2,1,0:T(8,128)(2,1)} %bitcast.293, bf16[24,5,128,128]{3,2,1,0:T(8,128)(2,1)} %copy-done), kind=kOutput, calls=%fused_computation.20 | convolution fusion | flops 615776256 | bytes 47972352 | tf_op jit(solution)/shard_map/dot_general | solution.py:55
  1061.3 49.0 %reduce.3 = bf16[3072,768]{1,0:T(8,128)(2,1)} reduce(bf16[3072,1,768]{2,1,0:T(2,128)(2,1)} %bitcast.301, bf16[]{:T(256)} %broadcast.90), dimensions={1}, to_apply=%bitcast.281.reduce_sub_computation | reduce | bytes 9437186
  1115.9 58.4 %all_to_all.16 = bf16[4,2,294912]{2,1,0:T(2,128)(2,1)} all-to-all(bf16[4,2,294912]{2,1,0:T(2,128)(2,1)} %reshape.348), channel_id=1, replica_groups=mesh['img'=8,'slab'=4] {'slab'}, dimensions={0} | all-to-all | bytes 9437184 | tf_op jit(solution)/shard_map/all_to_all | solution.py:83
  1182.4 23.6 %copy.111 = f32[1,4,768,768]{2,3,1,0:T(8,128)} copy(bf16[1,4,768,768]{3,0,2,1:T(2,128)(2,1)} %bitcast.302) | data formatting | bytes 14155776 | tf_op jit(solution)/shard_map/convert_element_type | solution.py:89
  1245.5 16.8 add_convert_fusion.1
  1275.3 25.0 %collective-permute-done.9 = bf16[1,768,768]{2,1,0:T(8,128)(2,1)S(1)} collective-permute-done((bf16[1,768,768]{2,1,0:T(8,128)(2,1)}, bf16[1,768,768]{2,1,0:T(8,128)(2,1)S(1)}, u32[]{:S(2)}, u32[]{:S(2)}) %collective-permute-start.9) | collective-permute-done | bytes 1179680 | tf_op jit(solution)/shard_map/ppermute | solution.py:78
  1300.3 20.7 %collective-permute-done.10 = bf16[1,768,768]{2,1,0:T(8,128)(2,1)} collective-permute-done((bf16[1,768,768]{2,1,0:T(8,128)(2,1)}, bf16[1,768,768]{2,1,0:T(8,128)(2,1)}, u32[]{:S(2)}, u32[]{:S(2)}) %collective-permute-start.10) | collective-permute-done | bytes 1179680 | tf_op jit(solution)/shard_map/ppermute | solution.py:78
  1360.4 18.2 %add_convert_fusion = bf16[24,128,768]{2,1,0:T(8,128)(2,1)} fusion(f32[24,128,768]{2,1,0:T(8,128)} %fusion.64, f32[24,128,768]{2,1,0:T(8,128)} %fusion.60, f32[24,128,768]{2,1,0:T(8,128)} %fusion.52, f32[24,128,768]{2,1,0:T(8,128)} %fusion.56, bf16[24,128,768]{2,1,0:T(8,128)(2,1)} %bitcast.287, bf16[24,5,128,128]{3,2,1,0:T(8,128)(2,1)} %copy-done), kind=kOutput, calls=%fused_computation.18 | convolution fusion | flops 615776256 | bytes 47972352 | tf_op jit(solution)/shard_map/dot_general | solution.py:55
  1388.1 49.2 %reduce.4 = bf16[3072,768]{1,0:T(8,128)(2,1)} reduce(bf16[3072,1,768]{2,1,0:T(2,128)(2,1)} %bitcast.298, bf16[]{:T(256)} %broadcast.90), dimensions={1}, to_apply=%bitcast.280.reduce_sub_computation | reduce | bytes 9437186
  1442.7 56.6 %all_to_all.17 = bf16[4,2,294912]{2,1,0:T(2,128)(2,1)} all-to-all(bf16[4,2,294912]{2,1,0:T(2,128)(2,1)} %reshape.350), channel_id=1, replica_groups=mesh['img'=8,'slab'=4] {'slab'}, dimensions={0} | all-to-all | bytes 9437184 | tf_op jit(solution)/shard_map/all_to_all | solution.py:83
  1522.6 23.3 %copy.119 = f32[1,4,768,768]{2,3,1,0:T(8,128)} copy(f32[1,4,768,768]{3,0,2,1:T(1,128)} %bitcast.303) | data formatting | bytes 18874368 | tf_op jit(solution)/shard_map/i,irc->rc/dot_general | solution.py:91
  1545.9 23.5 %copy.120 = f32[1,4,768,768]{2,3,1,0:T(8,128)} copy(bf16[1,4,768,768]{3,0,2,1:T(2,128)(2,1)} %bitcast.285) | data formatting | bytes 14155776 | tf_op jit(solution)/shard_map/convert_element_type | solution.py:91
  1569.4 172.2 %all-reduce.13.cloned.1.call-done = f32[768,3072]{0,1:T(8,128)} async-done(((f32[768,3072]{0,1:T(8,128)}), f32[768,3072]{0,1:T(8,128)}) %all-reduce.13.cloned.1.call-update) | async-done | bytes 9437200 | tf_op jit(solution)/shard_map/psum | solution.py:92
  (148 shorter events, 561.3 us)
Async XLA Ops:
  15.6 6.9 copy-start.12
  26.3 19.0 %copy-start = (bf16[24,5,128,128]{3,2,1,0:T(8,128)(2,1)}, bf16[24,5,128,128]{3,2,1,0:T(8,128)(2,1)S(1)}, u32[]{:S(2)}) copy-start(bf16[24,5,128,128]{3,2,1,0:T(8,128)(2,1)S(1)} %select_reduce_fusion) | copy-start | bytes 11796484
  26.3 8.9 copy-start.8
  73.2 30.1 %collective-permute-start = (bf16[1,768,768]{2,1,0:T(8,128)(2,1)}, bf16[1,768,768]{2,1,0:T(8,128)(2,1)}, u32[]{:S(2)}, u32[]{:S(2)}) collective-permute-start(bf16[1,768,768]{2,1,0:T(8,128)(2,1)} %bitcast.344), channel_id=1, source_target_pairs={{0,1},{1,0},{2,3},{3,2},{4,5},{5,4},{6,7},{7,6},{8,9},{9,8},{10,11... | collective-permute-start | bytes 3538952 | tf_op jit(solution)/shard_map/ppermute | solution.py:78
  77.7 52.9 %collective-permute-start.1 = (bf16[1,768,768]{2,1,0:T(8,128)(2,1)}, bf16[1,768,768]{2,1,0:T(8,128)(2,1)S(1)}, u32[]{:S(2)}, u32[]{:S(2)}) collective-permute-start(bf16[1,768,768]{2,1,0:T(8,128)(2,1)} %bitcast.345), channel_id=1, source_target_pairs={{0,2},{1,3},{2,0},{3,1},{4,6},{5,7},{6,4},{7,5},{8,10},{9,11},{10,... | collective-permute-start | bytes 3538952 | tf_op jit(solution)/shard_map/ppermute | solution.py:78
  80.7 50.0 %collective-permute-start.2 = (bf16[1,768,768]{2,1,0:T(8,128)(2,1)}, bf16[1,768,768]{2,1,0:T(8,128)(2,1)}, u32[]{:S(2)}, u32[]{:S(2)}) collective-permute-start(bf16[1,768,768]{2,1,0:T(8,128)(2,1)} %bitcast.349), channel_id=1, source_target_pairs={{0,3},{1,2},{2,1},{3,0},{4,7},{5,6},{6,5},{7,4},{8,11},{9,10},{10,... | collective-permute-start | bytes 3538952 | tf_op jit(solution)/shard_map/ppermute | solution.py:78
  81.4 53.0 %copy-start.13 = (s32[1024]{0:T(1024)}, s32[1024]{0:T(1024)S(1)}, u32[]{:S(2)}) copy-start(s32[1024]{0:T(1024)S(1)} %pad_clamp_fusion) | copy-start | bytes 12292
  139.8 7.8 copy-start.1
  250.7 57.5 %all-to-all-start = ((bf16[4,2,294912]{2,1,0:T(2,128)(2,1)}), bf16[4,2,294912]{2,1,0:T(2,128)(2,1)}, u32[]{:S(2)}, u32[]{:S(2)}) async-start(bf16[4,2,294912]{2,1,0:T(2,128)(2,1)} %reshape.344), calls=%async_computation | async-start | bytes 9437184 | tf_op jit(solution)/shard_map/all_to_all | solution.py:83
  356.4 7.8 copy-start.2
  356.4 7.8 copy-start.9
  405.1 29.1 %collective-permute-start.3 = (bf16[1,768,768]{2,1,0:T(8,128)(2,1)}, bf16[1,768,768]{2,1,0:T(8,128)(2,1)S(1)}, u32[]{:S(2)}, u32[]{:S(2)}) collective-permute-start(bf16[1,768,768]{2,1,0:T(8,128)(2,1)} %bitcast.350), channel_id=1, source_target_pairs={{0,1},{1,0},{2,3},{3,2},{4,5},{5,4},{6,7},{7,6},{8,9},{9,8},{10,11... | collective-permute-start | bytes 3538952 | tf_op jit(solution)/shard_map/ppermute | solution.py:78
  406.5 51.1 %collective-permute-start.4 = (bf16[1,768,768]{2,1,0:T(8,128)(2,1)}, bf16[1,768,768]{2,1,0:T(8,128)(2,1)}, u32[]{:S(2)}, u32[]{:S(2)}) collective-permute-start(bf16[1,768,768]{2,1,0:T(8,128)(2,1)} %bitcast.346), channel_id=1, source_target_pairs={{0,2},{1,3},{2,0},{3,1},{4,6},{5,7},{6,4},{7,5},{8,10},{9,11},{10,... | collective-permute-start | bytes 3538952 | tf_op jit(solution)/shard_map/ppermute | solution.py:78
  407.1 50.5 %collective-permute-start.5 = (bf16[1,768,768]{2,1,0:T(8,128)(2,1)}, bf16[1,768,768]{2,1,0:T(8,128)(2,1)}, u32[]{:S(2)}, u32[]{:S(2)}) collective-permute-start(bf16[1,768,768]{2,1,0:T(8,128)(2,1)} %bitcast.341), channel_id=1, source_target_pairs={{0,3},{1,2},{2,1},{3,0},{4,7},{5,6},{6,5},{7,4},{8,11},{9,10},{10,... | collective-permute-start | bytes 3538952 | tf_op jit(solution)/shard_map/ppermute | solution.py:78
  466.9 7.9 copy-start.3
  577.2 55.8 %all-to-all-start.1 = ((bf16[4,2,294912]{2,1,0:T(2,128)(2,1)}), bf16[4,2,294912]{2,1,0:T(2,128)(2,1)}, u32[]{:S(2)}, u32[]{:S(2)}) async-start(bf16[4,2,294912]{2,1,0:T(2,128)(2,1)} %reshape.346), calls=%async_computation.1 | async-start | bytes 9437184 | tf_op jit(solution)/shard_map/all_to_all | solution.py:83
  582.2 293.9 %all-reduce.11.cloned.1.call-start = ((), (), s32[]{:S(2)}) async-start(), calls=%async_computation.4 | async-start | bytes 18874368 | tf_op jit(solution)/shard_map/psum | solution.py:92
  679.7 1061.8 %all-reduce.13.cloned.1.call-start = ((), (), s32[]{:S(2)}) async-start(), calls=%async_computation.5 | async-start | bytes 18874368 | tf_op jit(solution)/shard_map/psum | solution.py:92
  893.0 7.8 copy-start.4
  893.0 7.8 copy-start.10
  941.7 29.1 %collective-permute-start.6 = (bf16[1,768,768]{2,1,0:T(8,128)(2,1)}, bf16[1,768,768]{2,1,0:T(8,128)(2,1)S(1)}, u32[]{:S(2)}, u32[]{:S(2)}) collective-permute-start(bf16[1,768,768]{2,1,0:T(8,128)(2,1)} %bitcast.351), channel_id=1, source_target_pairs={{0,1},{1,0},{2,3},{3,2},{4,5},{5,4},{6,7},{7,6},{8,9},{9,8},{10,11... | collective-permute-start | bytes 3538952 | tf_op jit(solution)/shard_map/ppermute | solution.py:78
  943.2 52.9 %collective-permute-start.7 = (bf16[1,768,768]{2,1,0:T(8,128)(2,1)}, bf16[1,768,768]{2,1,0:T(8,128)(2,1)}, u32[]{:S(2)}, u32[]{:S(2)}) collective-permute-start(bf16[1,768,768]{2,1,0:T(8,128)(2,1)} %bitcast.347), channel_id=1, source_target_pairs={{0,2},{1,3},{2,0},{3,1},{4,6},{5,7},{6,4},{7,5},{8,10},{9,11},{10,... | collective-permute-start | bytes 3538952 | tf_op jit(solution)/shard_map/ppermute | solution.py:78
  944.7 51.4 %collective-permute-start.8 = (bf16[1,768,768]{2,1,0:T(8,128)(2,1)}, bf16[1,768,768]{2,1,0:T(8,128)(2,1)}, u32[]{:S(2)}, u32[]{:S(2)}) collective-permute-start(bf16[1,768,768]{2,1,0:T(8,128)(2,1)} %bitcast.342), channel_id=1, source_target_pairs={{0,3},{1,2},{2,1},{3,0},{4,7},{5,6},{6,5},{7,4},{8,11},{9,10},{10,... | collective-permute-start | bytes 3538952 | tf_op jit(solution)/shard_map/ppermute | solution.py:78
  1005.2 8.1 copy-start.5
  1222.5 7.8 copy-start.6
  1222.5 7.8 copy-start.11
  1271.2 29.1 %collective-permute-start.9 = (bf16[1,768,768]{2,1,0:T(8,128)(2,1)}, bf16[1,768,768]{2,1,0:T(8,128)(2,1)S(1)}, u32[]{:S(2)}, u32[]{:S(2)}) collective-permute-start(bf16[1,768,768]{2,1,0:T(8,128)(2,1)} %bitcast.352), channel_id=1, source_target_pairs={{0,1},{1,0},{2,3},{3,2},{4,5},{5,4},{6,7},{7,6},{8,9},{9,8},{10,11... | collective-permute-start | bytes 3538952 | tf_op jit(solution)/shard_map/ppermute | solution.py:78
  1272.1 48.9 %collective-permute-start.10 = (bf16[1,768,768]{2,1,0:T(8,128)(2,1)}, bf16[1,768,768]{2,1,0:T(8,128)(2,1)}, u32[]{:S(2)}, u32[]{:S(2)}) collective-permute-start(bf16[1,768,768]{2,1,0:T(8,128)(2,1)} %bitcast.348), channel_id=1, source_target_pairs={{0,2},{1,3},{2,0},{3,1},{4,6},{5,7},{6,4},{7,5},{8,10},{9,11},{10,... | collective-permute-start | bytes 3538952 | tf_op jit(solution)/shard_map/ppermute | solution.py:78
  1272.7 50.0 %collective-permute-start.11 = (bf16[1,768,768]{2,1,0:T(8,128)(2,1)}, bf16[1,768,768]{2,1,0:T(8,128)(2,1)}, u32[]{:S(2)}, u32[]{:S(2)}) collective-permute-start(bf16[1,768,768]{2,1,0:T(8,128)(2,1)} %bitcast.343), channel_id=1, source_target_pairs={{0,3},{1,2},{2,1},{3,0},{4,7},{5,6},{6,5},{7,4},{8,11},{9,10},{10,... | collective-permute-start | bytes 3538952 | tf_op jit(solution)/shard_map/ppermute | solution.py:78
  1332.3 7.8 copy-start.7
Sparse Core Ops, SparseCore 0:
  679.8 196.1 all-reduce.10
  1546.0 195.4 all-reduce.12
